TPU v7x, 32 devices: a whole 2x2x4 slice. The times are simulated.
32 devices in a mesh: grp: 2 (over y), ctx: 8 (over z, x), pair: 2 (over core).
Axes of the slice: x: 2, y: 2, z: 4, core: 2. Of those that a mesh axis runs over, the one named last changes fastest.
Arguments:
- normed_input: bfloat16 [4, 1024, 2688], P(('grp', 'pair'), 'ctx'), parts along dimension 0, may hold values from -6 to 6
- queries: bfloat16 [4, 1024, 2048], P(('grp', 'pair'), 'ctx'), parts along dimension 0, may hold values from -64 to 64
- keys: bfloat16 [4, 1024, 1024], P(('grp', 'pair'), 'ctx'), parts along dimension 0, may hold values from -64 to 64
- value_projection: bfloat16 [2688, 1024], P('ctx'), may hold values from -0.125 to 0.125
- adapter_down: bfloat16 [2688, 16], replicated, may hold values from -0.125 to 0.125
- adapter_up: bfloat16 [16, 1024], replicated, may hold values from -1.5 to 1.5
- output_gradient: bfloat16 [4, 1024, 2048], P(('grp', 'pair'), 'ctx'), parts along dimension 0, may hold values from -6 to 6
- policy_logprob: float32 [4, 1024], P(('grp', 'pair'), 'ctx'), parts along dimension 0, may hold values from -6 to 0
- reference_logprob: float32 [4, 1024], P(('grp', 'pair'), 'ctx'), parts along dimension 0, may hold values from -8 to 0
- token_pair_index: int32 [4, 1024], P(('grp', 'pair'), 'ctx'), parts along dimension 0, may hold values from 0 to 7, never falling along the last dimension, each value on 1 to 1017 neighbouring positions
Outputs:
- input_grad: bfloat16 [4, 1024, 2688], P(('grp', 'pair'), 'ctx'), parts along dimension 0
- query_grad: bfloat16 [4, 1024, 2048], P(('grp', 'pair'), 'ctx'), parts along dimension 0
- key_grad: bfloat16 [4, 1024, 1024], P(('grp', 'pair'), 'ctx'), parts along dimension 0
- down_gradient: float32 [5376, 16], P('grp'), parts along dimension 0
- up_gradient: float32 [32, 1024], P('grp'), parts along dimension 0
There are 2 independent parts, one for each index of `grp`. A program takes and returns all parts, laid end to end along the dimension named above; an argument that names none is the same for every part. Nothing has to cross between parts.
Inputs may be any that keep to these rules, and one draw needn't show every extreme that they name: `token_pair_index`: along each sequence the ids never fall; both sequences hold every id, each segment at most 1017 tokens and one exactly 1017.
All inputs are finite; a program needn't handle non-finite values.
Results may differ from a plain program's by a relative error of at most 0.03.
Values may be sent and summed in bfloat16 or wider, within the bound.
No kernel may reach another device: no remote copies, remote signals or barrier semaphores. Data moves between devices by JAX's collectives and lax.ppermute only.
A program may use at most 128 MiB of HBM per device.

v0:
```python
import jax
import jax.numpy as jnp
from jax import lax
from jax.sharding import PartitionSpec as P

HEAD_SIZE = 128
WINDOW = 1024
SEGS = 8
DPO_BETA = 0.1
LOSS_SCALE = 256.0
ADAPTER_SCALE = 2.0
ATTN_SCALE = 168.0 ** (-0.5)
NEG_FILL = -1e30


def from_partner(shard, axis, stride):
    return lax.ppermute(shard, axis, [(i, i ^ 1 << stride) for i in range(lax.axis_size(axis))])


def shifted(block, axis, distance):
    devices = range(lax.axis_size(axis))
    route = [(i - distance, i) for i in devices if i - distance in devices]
    return lax.ppermute(block, axis, route)


def shards(
    normed_input,
    queries,
    keys,
    value_projection,
    adapter_down,
    adapter_up,
    output_gradient,
    policy_logprob,
    reference_logprob,
    token_pair_index,
):
    tok_rows = normed_input.shape[1]
    width_kv = keys.shape[2]
    kv_heads = width_kv // HEAD_SIZE
    group_size = queries.shape[2] // width_kv
    hidden_rows = normed_input[0]
    own_keys = keys[0]
    pair_index = lax.axis_index("pair")
    ctx_index = lax.axis_index("ctx")
    half_cols = width_kv // 2
    own_half = lax.dynamic_slice_in_dim(value_projection, pair_index * half_cols, half_cols, 1)
    rows_half = lax.all_gather(own_half, "ctx", axis=0, tiled=True)
    full_weight = lax.all_gather(rows_half, "pair", axis=1, tiled=True)
    rank_projection = jnp.dot(hidden_rows, adapter_down, preferred_element_type=jnp.float32).astype(
        jnp.bfloat16
    )
    values = (
        jnp.dot(hidden_rows, full_weight, preferred_element_type=jnp.float32)
        + ADAPTER_SCALE * jnp.dot(rank_projection, adapter_up, preferred_element_type=jnp.float32)
    ).astype(jnp.bfloat16)
    segment_labels = token_pair_index[0]
    seg_table = (segment_labels[:, None] == jnp.arange(SEGS, dtype=jnp.int32)[None, :]).astype(
        jnp.float32
    )
    log_gap = policy_logprob[0] - reference_logprob[0]
    part_diff = jnp.sum(seg_table * log_gap[:, None], 0)
    part_count = jnp.sum(seg_table, 0)
    own_diff, counts = lax.psum((part_diff, part_count), "ctx")
    other_diff = from_partner(own_diff, "pair", 0)
    direction = 1.0 - 2.0 * pair_index.astype(jnp.float32)
    margin = DPO_BETA * (direction * (own_diff - other_diff))
    coef = -direction * DPO_BETA * LOSS_SCALE * jax.nn.sigmoid(-margin)
    starts = jnp.cumsum(counts) - counts
    tok_start = jnp.sum(seg_table * starts[None, :], 1).astype(jnp.int32)
    token_coefficient = jnp.sum(seg_table * coef[None, :], 1)
    halo_blocks = min(WINDOW // tok_rows, lax.axis_size("ctx") - 1)
    key_blocks = []
    value_blocks = []
    for distance in range(halo_blocks, 0, -1):
        key_blocks.append(shifted(own_keys, "ctx", distance))
        value_blocks.append(shifted(values, "ctx", distance))
    all_keys = jnp.concatenate(key_blocks + [own_keys], 0)
    all_keys, own_values = lax.optimization_barrier((all_keys, values))
    all_values = jnp.concatenate(value_blocks + [own_values], 0)
    span = all_keys.shape[0]
    tpos = ctx_index * tok_rows + jnp.arange(tok_rows, dtype=jnp.int32)
    upos = ctx_index * tok_rows - halo_blocks * tok_rows + jnp.arange(span, dtype=jnp.int32)
    allowed = (
        (upos[None, :] <= tpos[:, None])
        & (upos[None, :] > tpos[:, None] - WINDOW)
        & (upos[None, :] >= tok_start[:, None])
    )
    coef_rows = token_coefficient[None, :, None]
    query_rows = queries[0].reshape(tok_rows, kv_heads, group_size, HEAD_SIZE)
    grad_rows = output_gradient[0].reshape(tok_rows, kv_heads, group_size, HEAD_SIZE)
    key_rows = all_keys.reshape(span, kv_heads, HEAD_SIZE)
    value_rows = all_values.reshape(span, kv_heads, HEAD_SIZE)
    scores = ATTN_SCALE * jnp.einsum(
        "tjgd,ljd->jgtl", query_rows, key_rows, preferred_element_type=jnp.float32
    )
    masked = jnp.where(allowed[None, None], scores, NEG_FILL)
    row_max = jnp.max(masked, -1, keepdims=True)
    weights_exp = jnp.where(allowed[None, None], jnp.exp(masked - row_max), 0.0)
    attn_probs = weights_exp / jnp.sum(weights_exp, -1, keepdims=True)
    prob_grad = coef_rows[None] * jnp.einsum(
        "tjgd,ljd->jgtl", grad_rows, value_rows, preferred_element_type=jnp.float32
    )
    row_delta = jnp.sum(attn_probs * prob_grad, -1, keepdims=True)
    score_grad = (ATTN_SCALE * attn_probs * (prob_grad - row_delta)).astype(jnp.bfloat16)
    query_grad = (
        jnp.einsum("jgtl,ljd->tjgd", score_grad, key_rows, preferred_element_type=jnp.float32)
        .astype(jnp.bfloat16)
        .reshape(tok_rows, kv_heads * group_size * HEAD_SIZE)
    )
    key_parts = jnp.einsum(
        "jgtl,tjgd->ljd", score_grad, query_rows, preferred_element_type=jnp.float32
    ).reshape(span, width_kv)
    weighted = (attn_probs * coef_rows[None]).astype(jnp.bfloat16)
    value_parts = jnp.einsum(
        "jgtl,tjgd->ljd", weighted, grad_rows, preferred_element_type=jnp.float32
    ).reshape(span, width_kv)
    key_total = key_parts[halo_blocks * tok_rows :]
    value_total = value_parts[halo_blocks * tok_rows :]
    for distance in range(1, halo_blocks + 1):
        block_start = (halo_blocks - distance) * tok_rows
        send_keys = key_parts[block_start : block_start + tok_rows].astype(jnp.bfloat16)
        send_values = value_parts[block_start : block_start + tok_rows].astype(jnp.bfloat16)
        back_keys, back_values = shifted((send_keys, send_values), "ctx", -distance)
        key_total = key_total + back_keys.astype(jnp.float32)
        value_total = value_total + back_values.astype(jnp.float32)
    key_grad = key_total.astype(jnp.bfloat16)
    value_gradient = value_total.astype(jnp.bfloat16)
    rank_middle = jnp.einsum(
        "sj,zj->sz", value_gradient, adapter_up, preferred_element_type=jnp.float32
    ).astype(jnp.bfloat16)
    input_grad = (
        jnp.einsum("tk,dk->td", value_gradient, full_weight, preferred_element_type=jnp.float32)
        + ADAPTER_SCALE
        * jnp.einsum("pb,wb->pw", rank_middle, adapter_down, preferred_element_type=jnp.float32)
    ).astype(jnp.bfloat16)
    up_factor = ADAPTER_SCALE * jnp.einsum(
        "tr,tk->rk", rank_projection, value_gradient, preferred_element_type=jnp.float32
    )
    down_factor = ADAPTER_SCALE * jnp.einsum(
        "td,tr->dr", hidden_rows, rank_middle, preferred_element_type=jnp.float32
    )
    down_gradient, up_gradient = lax.psum((down_factor, up_factor), ("ctx", "pair"))
    return (input_grad[None], query_grad[None], key_grad[None], down_gradient, up_gradient)


def solution(mesh):
    return jax.shard_map(
        shards,
        mesh=mesh,
        in_specs=(
            P(("grp", "pair"), "ctx", None),
            P(("grp", "pair"), "ctx", None),
            P(("grp", "pair"), "ctx", None),
            P("ctx", None),
            P(),
            P(),
            P(("grp", "pair"), "ctx", None),
            P(("grp", "pair"), "ctx"),
            P(("grp", "pair"), "ctx"),
            P(("grp", "pair"), "ctx"),
        ),
        out_specs=(
            P(("grp", "pair"), "ctx", None),
            P(("grp", "pair"), "ctx", None),
            P(("grp", "pair"), "ctx", None),
            P("grp", None),
            P("grp", None),
        ),
        check_vma=False,
    )
```

profile of v0, /device:TPU:8, one launch (start us, length us, event | category | flops | bytes accessed | tf_op | source)
XLA Modules:
  0.0 361.4 jit_solution(16586474015925666652)
XLA Ops:
  9.2 58.9 %all-gather.3.cloned.1.call-done = bf16[2688,512]{1,0:T(8,128)(2,1)} async-done(((bf16[336,512]{1,0:T(8,128)(2,1)}), bf16[2688,512]{1,0:T(8,128)(2,1)}) %all-gather.3.cloned.1.call-update) | async-done | bytes 2752528 | tf_op jit(solution)/shard_map/all_gather | solution.py:48
  70.2 4.2 %collective-permute-start.2 = (bf16[128,1024]{1,0:T(8,128)(2,1)}, bf16[128,1024]{1,0:T(8,128)(2,1)}, u32[]{:S(2)}, u32[]{:S(2)}) collective-permute-start(bf16[128,1024]{1,0:T(8,128)(2,1)} %bitcast.3), channel_id=1, source_target_pairs={{0,10},{2,12},{4,14},{1,11},{3,13},{5,15},{16,26},{18,28},{20,30},... | collective-permute-start | bytes 786440 | tf_op jit(solution)/shard_map/ppermute | solution.py:23
  76.5 30.3 %all-reduce.1 = (f32[8]{0:T(128)S(1)}, f32[8]{0:T(128)S(1)}) all-reduce(f32[8]{0:T(128)S(1)} %get-tuple-element.21, f32[8]{0:T(128)S(1)} %get-tuple-element.22), channel_id=1, replica_groups=mesh['grp'=2,'ctx'=8,'pair'=2] {'ctx'}, use_global_device_ids=true, to_apply=%region_1.0 | all-reduce | flops 16 | bytes 128 | tf_op jit(solution)/shard_map/psum | solution.py:64
  108.8 2.9 collective-permute-start.4
  113.4 3.2 collective-permute-start.5
  122.4 3.8 %collective-permute-done.5 = bf16[128,1024]{1,0:T(8,128)(2,1)S(1)} collective-permute-done((bf16[128,1024]{1,0:T(8,128)(2,1)}, bf16[128,1024]{1,0:T(8,128)(2,1)S(1)}, u32[]{:S(2)}, u32[]{:S(2)}) %collective-permute-start.5) | collective-permute-done | bytes 262176 | tf_op jit(solution)/shard_map/ppermute | solution.py:23
  126.3 4.2 %collective-permute-done.6 = bf16[128,1024]{1,0:T(8,128)(2,1)S(1)} collective-permute-done((bf16[128,1024]{1,0:T(8,128)(2,1)}, bf16[128,1024]{1,0:T(8,128)(2,1)S(1)}, u32[]{:S(2)}, u32[]{:S(2)}) %collective-permute-start.6) | collective-permute-done | bytes 262176 | tf_op jit(solution)/shard_map/ppermute | solution.py:23
  131.5 4.2 %convolution_bitcast_fusion.1 = f32[128,1024]{0,1:T(8,128)S(1)} fusion(bf16[2688,1024]{1,0:T(8,128)(2,1)} %all-gather.5.cloned.1.call-done, bf16[1,128,2688]{2,1,0:T(8,128)(2,1)S(1)} %copy-done), kind=kOutput, calls=%fused_computation.26 | convolution fusion | flops 704643072 | bytes 6717440 | tf_op jit(solution)/shard_map/dot_general | solution.py:54
  139.4 2.3 collective-permute-start.17
  141.6 6.5 %collective-permute-start.18 = (bf16[128,1024]{0,1:T(8,128)(2,1)}, bf16[128,1024]{0,1:T(8,128)(2,1)}, u32[]{:S(2)}, u32[]{:S(2)}) collective-permute-start(bf16[128,1024]{0,1:T(8,128)(2,1)} %fusion.15), channel_id=1, source_target_pairs={{0,8},{2,10},{4,12},{6,14},{1,9},{3,11},{5,13},{7,15},{16,24},{18,... | collective-permute-start | bytes 786440 | tf_op jit(solution)/shard_map/ppermute | solution.py:23
  152.1 3.2 copy.60
  155.4 6.9 %fusion.36 = (f32[8,2,128]{2,1,0:T(2,128)S(1)}, f32[8,2,128,1024]{2,3,1,0:T(8,128)}) fusion(pred[128,1024]{0,1:T(8,128)(4,1)} %compare_and_fusion, bf16[1024,8,128,1]{0,2,3,1:T(8,128)(2,1)S(1)} %copy.60, bf16[128,8,2,128]{0,3,2,1:T(8,128)(2,1)S(1)} %bitcast.126), kind=kOutput, calls=%fused_computation.82 | convolution fusion | flops 547357696 | bytes 11149312 | tf_op jit(solution)/shard_map/sub | solution.py:99
  162.3 5.1 %fusion.37 = (bf16[1024,8,128]{0,2,1:T(8,128)(2,1)S(1)}, f32[1024,8,128]{0,2,1:T(8,128)S(1)}) fusion(bf16[128,8,2,128]{3,2,1,0:T(2,128)(2,1)} %reshape_squeeze.7, f32[128]{0:T(128)S(1)} %get-tuple-element.20, f32[8,2,128,1024]{2,3,1,0:T(8,128)} %get-tuple-element.42, f32[8,2,128]{2,1,0:T(2,128)S(1)} %get-tuple-element.41), kind=kOutput, calls=%fused_computation.83 | convolution fusion | flops 544210944 | bytes 15213056 | tf_op jit(solution)/shard_map/jgtl,tjgd->ljd/dot_general | solution.py:115
  168.0 2.9 collective-permute-start.20
  180.8 3.2 collective-permute-done.20
  193.4 2.9 collective-permute-start.9
  196.3 3.1 collective-permute-start.8
  199.5 3.5 fusion.38
  203.1 19.5 %collective-permute-done.10 = bf16[128,1024]{0,1:T(8,128)(2,1)S(1)} collective-permute-done((bf16[128,1024]{0,1:T(8,128)(2,1)S(1)}, bf16[128,1024]{0,1:T(8,128)(2,1)S(1)}, u32[]{:S(2)}, u32[]{:S(2)}) %collective-permute-start.10) | collective-permute-done | bytes 262176 | tf_op jit(solution)/shard_map/ppermute | solution.py:23
  225.4 2.0 copy.54
  249.4 5.3 %fusion.11 = bf16[1,128,2688]{2,1,0:T(8,128)(2,1)} fusion(f32[128,2688]{1,0:T(8,128)S(1)} %convolution_multiply_fusion, bf16[128,1024]{0,1:T(8,128)(2,1)S(1)} %fusion.27, bf16[2688,1024]{1,0:T(8,128)(2,1)} %all-gather.5.cloned.1.call-done), kind=kOutput, calls=%fused_computation.19 | convolution fusion | flops 705331200 | bytes 7831552 | tf_op jit(solution)/shard_map/tk,dk->td/dot_general | solution.py:133
  254.7 16.3 %collective-permute-done.24 = bf16[128,1024]{1,0:T(8,128)(2,1)} collective-permute-done((bf16[128,1024]{1,0:T(8,128)(2,1)}, bf16[128,1024]{1,0:T(8,128)(2,1)}, u32[]{:S(2)}, u32[]{:S(2)}) %collective-permute-start.24) | collective-permute-done | bytes 262176 | tf_op jit(solution)/shard_map/ppermute | solution.py:23
  271.1 3.9 %collective-permute-done.23 = bf16[128,1024]{1,0:T(8,128)(2,1)S(1)} collective-permute-done((bf16[128,1024]{1,0:T(8,128)(2,1)}, bf16[128,1024]{1,0:T(8,128)(2,1)S(1)}, u32[]{:S(2)}, u32[]{:S(2)}) %collective-permute-start.23) | collective-permute-done | bytes 262176 | tf_op jit(solution)/shard_map/ppermute | solution.py:23
  277.0 74.8 %all-reduce.4.cloned.1.call-done = (f32[2688,16]{0,1:T(8,128)}, f32[16,1024]{1,0:T(8,128)}) async-done(((f32[2688,16]{0,1:T(8,128)}, f32[16,1024]{1,0:T(8,128)}), (f32[2688,16]{0,1:T(8,128)}, f32[16,1024]{1,0:T(8,128)})) %all-reduce.4.cloned.1.call-update) | async-done | bytes 237584 | tf_op jit(solution)/shard_map/psum | solution.py:143
  (137 shorter events, 73.9 us)
Async XLA Ops:
  7.2 60.8 %all-gather.3.cloned.1.call-start = ((), (), s32[]{:S(2)}) async-start(), calls=%async_computation | async-start | bytes 3096576 | tf_op jit(solution)/shard_map/all_gather | solution.py:48
  9.1 122.3 %all-gather.5.cloned.1.call-start = ((), (), s32[]{:S(2)}) async-start(), calls=%async_computation.1 | async-start | bytes 8257536 | tf_op jit(solution)/shard_map/all_gather | solution.py:49
  68.1 283.8 %all-reduce.4.cloned.1.call-start = ((), (), s32[]{:S(2)}) async-start(), calls=%async_computation.2 | async-start | bytes 475136 | tf_op jit(solution)/shard_map/psum | solution.py:143
  68.1 44.5 %collective-permute-start = (bf16[128,1024]{1,0:T(8,128)(2,1)}, bf16[128,1024]{1,0:T(8,128)(2,1)S(1)}, u32[]{:S(2)}, u32[]{:S(2)}) collective-permute-start(bf16[128,1024]{1,0:T(8,128)(2,1)} %bitcast.3), channel_id=1, source_target_pairs={{0,14},{1,15},{16,30},{17,31}} | collective-permute-start | bytes 786440 | tf_op jit(solution)/shard_map/ppermute | solution.py:23
  68.8 48.7 %collective-permute-start.1 = (bf16[128,1024]{1,0:T(8,128)(2,1)}, bf16[128,1024]{1,0:T(8,128)(2,1)}, u32[]{:S(2)}, u32[]{:S(2)}) collective-permute-start(bf16[128,1024]{1,0:T(8,128)(2,1)} %bitcast.3), channel_id=1, source_target_pairs={{0,12},{2,14},{1,13},{3,15},{16,28},{18,30},{17,29},{19,31}} | collective-permute-start | bytes 786440 | tf_op jit(solution)/shard_map/ppermute | solution.py:23
  70.2 50.3 %collective-permute-start.2 = (bf16[128,1024]{1,0:T(8,128)(2,1)}, bf16[128,1024]{1,0:T(8,128)(2,1)}, u32[]{:S(2)}, u32[]{:S(2)}) collective-permute-start(bf16[128,1024]{1,0:T(8,128)(2,1)} %bitcast.3), channel_id=1, source_target_pairs={{0,10},{2,12},{4,14},{1,11},{3,13},{5,15},{16,26},{18,28},{20,30},... | collective-permute-start | bytes 786440 | tf_op jit(solution)/shard_map/ppermute | solution.py:23
  74.3 47.1 %collective-permute-start.3 = (bf16[128,1024]{1,0:T(8,128)(2,1)}, bf16[128,1024]{1,0:T(8,128)(2,1)}, u32[]{:S(2)}, u32[]{:S(2)}) collective-permute-start(bf16[128,1024]{1,0:T(8,128)(2,1)} %bitcast.3), channel_id=1, source_target_pairs={{0,8},{2,10},{4,12},{6,14},{1,9},{3,11},{5,13},{7,15},{16,24},{18,... | collective-permute-start | bytes 786440 | tf_op jit(solution)/shard_map/ppermute | solution.py:23
  136.7 31.4 %collective-permute-start.15 = (bf16[128,1024]{0,1:T(8,128)(2,1)}, bf16[128,1024]{0,1:T(8,128)(2,1)}, u32[]{:S(2)}, u32[]{:S(2)}) collective-permute-start(bf16[128,1024]{0,1:T(8,128)(2,1)} %fusion.15), channel_id=1, source_target_pairs={{0,14},{1,15},{16,30},{17,31}} | collective-permute-start | bytes 786440 | tf_op jit(solution)/shard_map/ppermute | solution.py:23
  138.0 34.0 %collective-permute-start.16 = (bf16[128,1024]{0,1:T(8,128)(2,1)}, bf16[128,1024]{0,1:T(8,128)(2,1)}, u32[]{:S(2)}, u32[]{:S(2)}) collective-permute-start(bf16[128,1024]{0,1:T(8,128)(2,1)} %fusion.15), channel_id=1, source_target_pairs={{0,12},{2,14},{1,13},{3,15},{16,28},{18,30},{17,29},{19,31}} | collective-permute-start | bytes 786440 | tf_op jit(solution)/shard_map/ppermute | solution.py:23
  139.4 35.6 %collective-permute-start.17 = (bf16[128,1024]{0,1:T(8,128)(2,1)}, bf16[128,1024]{0,1:T(8,128)(2,1)}, u32[]{:S(2)}, u32[]{:S(2)}) collective-permute-start(bf16[128,1024]{0,1:T(8,128)(2,1)} %fusion.15), channel_id=1, source_target_pairs={{0,10},{2,12},{4,14},{1,11},{3,13},{5,15},{16,26},{18,28},{20,30},... | collective-permute-start | bytes 786440 | tf_op jit(solution)/shard_map/ppermute | solution.py:23
  141.6 35.1 %collective-permute-start.18 = (bf16[128,1024]{0,1:T(8,128)(2,1)}, bf16[128,1024]{0,1:T(8,128)(2,1)}, u32[]{:S(2)}, u32[]{:S(2)}) collective-permute-start(bf16[128,1024]{0,1:T(8,128)(2,1)} %fusion.15), channel_id=1, source_target_pairs={{0,8},{2,10},{4,12},{6,14},{1,9},{3,11},{5,13},{7,15},{16,24},{18,... | collective-permute-start | bytes 786440 | tf_op jit(solution)/shard_map/ppermute | solution.py:23
  148.2 30.3 %collective-permute-start.19 = (bf16[128,1024]{0,1:T(8,128)(2,1)}, bf16[128,1024]{0,1:T(8,128)(2,1)}, u32[]{:S(2)}, u32[]{:S(2)}) collective-permute-start(bf16[128,1024]{0,1:T(8,128)(2,1)} %fusion.15), channel_id=1, source_target_pairs={{0,6},{2,8},{4,10},{6,12},{8,14},{1,7},{3,9},{5,11},{7,13},{9,15},... | collective-permute-start | bytes 786440 | tf_op jit(solution)/shard_map/ppermute | solution.py:23
  175.0 18.5 %collective-permute-start.14 = (bf16[128,1024]{0,1:T(8,128)(2,1)S(1)}, bf16[128,1024]{0,1:T(8,128)(2,1)S(1)}, u32[]{:S(2)}, u32[]{:S(2)}) collective-permute-start(bf16[128,1024]{0,1:T(8,128)(2,1)S(1)} %bitcast.141), channel_id=1, source_target_pairs={{14,0},{15,1},{30,16},{31,17}} | collective-permute-start | bytes 786440 | tf_op jit(solution)/shard_map/ppermute | solution.py:23
  176.7 19.6 %collective-permute-start.13 = (bf16[128,1024]{0,1:T(8,128)(2,1)S(1)}, bf16[128,1024]{0,1:T(8,128)(2,1)S(1)}, u32[]{:S(2)}, u32[]{:S(2)}) collective-permute-start(bf16[128,1024]{0,1:T(8,128)(2,1)S(1)} %bitcast.140), channel_id=1, source_target_pairs={{12,0},{14,2},{13,1},{15,3},{28,16},{30,18},{29,17},{31,19}} | collective-permute-start | bytes 786440 | tf_op jit(solution)/shard_map/ppermute | solution.py:23
  178.4 24.5 %collective-permute-start.12 = (bf16[128,1024]{0,1:T(8,128)(2,1)S(1)}, bf16[128,1024]{0,1:T(8,128)(2,1)S(1)}, u32[]{:S(2)}, u32[]{:S(2)}) collective-permute-start(bf16[128,1024]{0,1:T(8,128)(2,1)S(1)} %bitcast.139), channel_id=1, source_target_pairs={{10,0},{12,2},{14,4},{11,1},{13,3},{15,5},{26,16},{28,18},{30,20},... | collective-permute-start | bytes 786440 | tf_op jit(solution)/shard_map/ppermute | solution.py:23
  184.0 19.2 %collective-permute-start.11 = (bf16[128,1024]{0,1:T(8,128)(2,1)S(1)}, bf16[128,1024]{0,1:T(8,128)(2,1)S(1)}, u32[]{:S(2)}, u32[]{:S(2)}) collective-permute-start(bf16[128,1024]{0,1:T(8,128)(2,1)S(1)} %bitcast.138), channel_id=1, source_target_pairs={{8,0},{10,2},{12,4},{14,6},{9,1},{11,3},{13,5},{15,7},{24,16},{26,... | collective-permute-start | bytes 786440 | tf_op jit(solution)/shard_map/ppermute | solution.py:23
  185.5 37.2 %collective-permute-start.10 = (bf16[128,1024]{0,1:T(8,128)(2,1)S(1)}, bf16[128,1024]{0,1:T(8,128)(2,1)S(1)}, u32[]{:S(2)}, u32[]{:S(2)}) collective-permute-start(bf16[128,1024]{0,1:T(8,128)(2,1)S(1)} %bitcast.137), channel_id=1, source_target_pairs={{6,0},{8,2},{10,4},{12,6},{14,8},{7,1},{9,3},{11,5},{13,7},{15,9},... | collective-permute-start | bytes 786440 | tf_op jit(solution)/shard_map/ppermute | solution.py:23
  193.4 30.7 %collective-permute-start.9 = (bf16[128,1024]{0,1:T(8,128)(2,1)S(1)}, bf16[128,1024]{0,1:T(8,128)(2,1)S(1)}, u32[]{:S(2)}, u32[]{:S(2)}) collective-permute-start(bf16[128,1024]{0,1:T(8,128)(2,1)S(1)} %bitcast.136), channel_id=1, source_target_pairs={{4,0},{6,2},{8,4},{10,6},{12,8},{14,10},{5,1},{7,3},{9,5},{11,7},{... | collective-permute-start | bytes 786440 | tf_op jit(solution)/shard_map/ppermute | solution.py:23
  196.3 27.8 %collective-permute-start.8 = (bf16[128,1024]{0,1:T(8,128)(2,1)S(1)}, bf16[128,1024]{0,1:T(8,128)(2,1)S(1)}, u32[]{:S(2)}, u32[]{:S(2)}) collective-permute-start(bf16[128,1024]{0,1:T(8,128)(2,1)S(1)} %bitcast.135), channel_id=1, source_target_pairs={{2,0},{4,2},{6,4},{8,6},{10,8},{12,10},{14,12},{3,1},{5,3},{7,5},{... | collective-permute-start | bytes 786440 | tf_op jit(solution)/shard_map/ppermute | solution.py:23
  235.7 19.1 %collective-permute-start.26 = (bf16[128,1024]{1,0:T(8,128)(2,1)}, bf16[128,1024]{1,0:T(8,128)(2,1)S(1)}, u32[]{:S(2)}, u32[]{:S(2)}) collective-permute-start(bf16[128,1024]{1,0:T(8,128)(2,1)} %copy.51), channel_id=1, source_target_pairs={{10,0},{12,2},{14,4},{11,1},{13,3},{15,5},{26,16},{28,18},{30,20},... | collective-permute-start | bytes 786440 | tf_op jit(solution)/shard_map/ppermute | solution.py:23
  238.7 16.0 %collective-permute-start.25 = (bf16[128,1024]{1,0:T(8,128)(2,1)}, bf16[128,1024]{1,0:T(8,128)(2,1)S(1)}, u32[]{:S(2)}, u32[]{:S(2)}) collective-permute-start(bf16[128,1024]{1,0:T(8,128)(2,1)} %copy.50), channel_id=1, source_target_pairs={{8,0},{10,2},{12,4},{14,6},{9,1},{11,3},{13,5},{15,7},{24,16},{26,... | collective-permute-start | bytes 786440 | tf_op jit(solution)/shard_map/ppermute | solution.py:23
  240.8 30.2 %collective-permute-start.24 = (bf16[128,1024]{1,0:T(8,128)(2,1)}, bf16[128,1024]{1,0:T(8,128)(2,1)}, u32[]{:S(2)}, u32[]{:S(2)}) collective-permute-start(bf16[128,1024]{1,0:T(8,128)(2,1)} %copy.49), channel_id=1, source_target_pairs={{6,0},{8,2},{10,4},{12,6},{14,8},{7,1},{9,3},{11,5},{13,7},{15,9},... | collective-permute-start | bytes 786440 | tf_op jit(solution)/shard_map/ppermute | solution.py:23
  245.5 29.5 %collective-permute-start.23 = (bf16[128,1024]{1,0:T(8,128)(2,1)}, bf16[128,1024]{1,0:T(8,128)(2,1)S(1)}, u32[]{:S(2)}, u32[]{:S(2)}) collective-permute-start(bf16[128,1024]{1,0:T(8,128)(2,1)} %copy.48), channel_id=1, source_target_pairs={{4,0},{6,2},{8,4},{10,6},{12,8},{14,10},{5,1},{7,3},{9,5},{11,7},{... | collective-permute-start | bytes 786440 | tf_op jit(solution)/shard_map/ppermute | solution.py:23
  247.4 27.6 %collective-permute-start.22 = (bf16[128,1024]{1,0:T(8,128)(2,1)}, bf16[128,1024]{1,0:T(8,128)(2,1)S(1)}, u32[]{:S(2)}, u32[]{:S(2)}) collective-permute-start(bf16[128,1024]{1,0:T(8,128)(2,1)} %copy.46), channel_id=1, source_target_pairs={{2,0},{4,2},{6,4},{8,6},{10,8},{12,10},{14,12},{3,1},{5,3},{7,5},{... | collective-permute-start | bytes 786440 | tf_op jit(solution)/shard_map/ppermute | solution.py:23
  (23 other events, 757.6 us)
Sparse Core Ops, SparseCore 0:
  10.8 57.1 all-gather.2
  69.6 14.4 all-gather.4
  245.2 106.5 all-reduce.3
where the time goes:
time: 363 us; the launch traced here: 361 us
  waiting for transfers between devices  187 us (52%)
  starting transfers between devices  55.1 us (15%)
  local copies, waits for them, and re-layouts  37.7 us (10%)
  matrix products  32 us (9%)
  blocking collectives  30.3 us (8%)
  between operations  14.4 us (4%)
  other arithmetic  5.29 us (1%)
    psum x1, waiting for transfers between devices, shards(): lax.psum((down_factor, up_factor), ('ctx', 'pair'))  74.8 us
    all_gather x1, waiting for transfers between devices, shards(): rows_half = lax.all_gather(own_half, 'ctx', axis=0, tiled=True)  58.9 us
    ppermute x28, starting transfers between devices, shifted(): return lax.ppermute(block, axis, route)  55 us
    ppermute x28, waiting for transfers between devices, shifted(): return lax.ppermute(block, axis, route)  52.8 us
    psum x1, blocking collectives, shards(): own_diff, counts = lax.psum((part_diff, part_count), 'ctx')  30.3 us
    unnamed x48, local copies, waits for them, and re-layouts  17.1 us
    convert_element_type x7, local copies, waits for them, and re-layouts, shards(): key_parts[block_start:block_start + tok_rows].astype(jnp.bfloat16)  8.84 us
  transfers between devices with their start and end apart: 32, of which 11 were waited for; matrix products, arithmetic and copies ran while one was open for 16% of the time, Pallas kernels for 0%

commit v1 on v0

--- a/solution.py
+++ b/solution.py
@@ -1,7 +1,9 @@
+import functools
 import jax
 import jax.numpy as jnp
 from jax import lax
 from jax.sharding import PartitionSpec as P
+from jax.lax import axis_index, axis_size, ppermute
 
 HEAD_SIZE = 128
 WINDOW = 1024
@@ -11,6 +13,23 @@
 ADAPTER_SCALE = 2.0
 ATTN_SCALE = 168.0 ** (-0.5)
 NEG_FILL = -1e30
+
+
+def try_all_tasks_by_axis(payload, named_axis, row_dim):
+    shelf = [payload]
+    dev_n = axis_size(named_axis)
+    for jj in range(dev_n - 1):
+        shelf.append(
+            ppermute(shelf[-1], named_axis, [(kk, (kk + 1) % dev_n) for kk in range(dev_n)])
+        )
+    return jnp.roll(
+        jnp.concatenate(shelf[::-1], axis=row_dim),
+        shift=(axis_index(named_axis) + 1) * payload.shape[row_dim],
+        axis=row_dim,
+    )
+
+
+begin_spots_for = functools.partial(try_all_tasks_by_axis, named_axis="ctx", row_dim=0)
 
 
 def from_partner(shard, axis, stride):
@@ -45,7 +64,7 @@
     ctx_index = lax.axis_index("ctx")
     half_cols = width_kv // 2
     own_half = lax.dynamic_slice_in_dim(value_projection, pair_index * half_cols, half_cols, 1)
-    rows_half = lax.all_gather(own_half, "ctx", axis=0, tiled=True)
+    rows_half = begin_spots_for(own_half)
     full_weight = lax.all_gather(rows_half, "pair", axis=1, tiled=True)
     rank_projection = jnp.dot(hidden_rows, adapter_down, preferred_element_type=jnp.float32).astype(
         jnp.bfloat16

time: 363 us -> 376 us (1.036)
  starting transfers between devices: 55.1 us -> 63.5 us
  local copies, waits for them, and re-layouts: 37.7 us -> 45.1 us
  blocking collectives: 30.3 us -> 23.9 us
    ppermute x0 -> x7, waiting for transfers between devices: none -> 65.9 us  [try_all_tasks_by_axis(): ppermute(shelf[-1], named_axis, [(kk, (kk + 1) % dev_n) for kk in range(d...]
    all_gather x1 -> x0, waiting for transfers between devices: 58.9 us -> none  [shards(): rows_half = lax.all_gather(own_half, 'ctx', axis=0, tiled=True)]
    psum x1, blocking collectives: 30.3 us -> 23.9 us  [shards(): own_diff, counts = lax.psum((part_diff, part_count), 'ctx')]
    ppermute x28, starting transfers between devices: 55 us -> 61 us  [shifted(): return lax.ppermute(block, axis, route)]
    unnamed x48 -> x59, local copies, waits for them, and re-layouts: 17.1 us -> 19.4 us
  transfers between devices with their start and end apart: 32 -> 38, of which waited for: 11 -> 17; matrix products, arithmetic and copies ran while one was open for 16% -> 16% of each run, Pallas kernels for 0% -> 0%
where the time goes in v1:
time: 376 us; the launch traced here: 375 us
  waiting for transfers between devices  190 us (51%)
  starting transfers between devices  63.5 us (17%)
  local copies, waits for them, and re-layouts  45.1 us (12%)
  matrix products  31.9 us (8%)
  blocking collectives  23.9 us (6%)
  between operations  14.8 us (4%)
  other arithmetic  5.23 us (1%)
    psum x1, waiting for transfers between devices, shards(): lax.psum((down_factor, up_factor), ('ctx', 'pair'))  73.1 us
    ppermute x7, waiting for transfers between devices, try_all_tasks_by_axis(): ppermute(shelf[-1], named_axis, [(kk, (kk + 1) % dev_n) for kk in range(d...  65.9 us
    ppermute x28, starting transfers between devices, shifted(): return lax.ppermute(block, axis, route)  61 us
    ppermute x28, waiting for transfers between devices, shifted(): return lax.ppermute(block, axis, route)  51.3 us
    psum x1, blocking collectives, shards(): own_diff, counts = lax.psum((part_diff, part_count), 'ctx')  23.9 us
    unnamed x59, local copies, waits for them, and re-layouts  19.4 us
    convert_element_type x7, local copies, waits for them, and re-layouts, shards(): key_parts[block_start:block_start + tok_rows].astype(jnp.bfloat16)  11.6 us
  transfers between devices with their start and end apart: 38, of which 17 were waited for; matrix products, arithmetic and copies ran while one was open for 16% of the time, Pallas kernels for 0%

profile of v1, /device:TPU:8, one launch (start us, length us, event | category | flops | bytes accessed | tf_op | source)
XLA Modules:
  0.0 374.8 jit_solution(16348364651502858130)
XLA Ops:
  9.9 9.2 %collective-permute-done.7 = bf16[336,512]{1,0:T(8,128)(2,1)S(1)} collective-permute-done((bf16[336,512]{1,0:T(8,128)(2,1)S(1)}, bf16[336,512]{1,0:T(8,128)(2,1)S(1)}, u32[]{:S(2)}, u32[]{:S(2)}) %collective-permute-start.7) | collective-permute-done | bytes 344096 | tf_op jit(solution)/shard_map/ppermute | solution.py:23
  19.7 9.2 %collective-permute-done.8 = bf16[336,512]{1,0:T(8,128)(2,1)S(1)} collective-permute-done((bf16[336,512]{1,0:T(8,128)(2,1)S(1)}, bf16[336,512]{1,0:T(8,128)(2,1)S(1)}, u32[]{:S(2)}, u32[]{:S(2)}) %collective-permute-start.8) | collective-permute-done | bytes 344096 | tf_op jit(solution)/shard_map/ppermute | solution.py:23
  28.9 8.9 %collective-permute-done.9 = bf16[336,512]{1,0:T(8,128)(2,1)S(1)} collective-permute-done((bf16[336,512]{1,0:T(8,128)(2,1)S(1)}, bf16[336,512]{1,0:T(8,128)(2,1)S(1)}, u32[]{:S(2)}, u32[]{:S(2)}) %collective-permute-start.9) | collective-permute-done | bytes 344096 | tf_op jit(solution)/shard_map/ppermute | solution.py:23
  37.8 9.5 %collective-permute-done.10 = bf16[336,512]{1,0:T(8,128)(2,1)S(1)} collective-permute-done((bf16[336,512]{1,0:T(8,128)(2,1)S(1)}, bf16[336,512]{1,0:T(8,128)(2,1)S(1)}, u32[]{:S(2)}, u32[]{:S(2)}) %collective-permute-start.10) | collective-permute-done | bytes 344096 | tf_op jit(solution)/shard_map/ppermute | solution.py:23
  47.4 9.4 %collective-permute-done.11 = bf16[336,512]{1,0:T(8,128)(2,1)S(1)} collective-permute-done((bf16[336,512]{1,0:T(8,128)(2,1)S(1)}, bf16[336,512]{1,0:T(8,128)(2,1)S(1)}, u32[]{:S(2)}, u32[]{:S(2)}) %collective-permute-start.11) | collective-permute-done | bytes 344096 | tf_op jit(solution)/shard_map/ppermute | solution.py:23
  56.8 9.7 %collective-permute-done.12 = bf16[336,512]{1,0:T(8,128)(2,1)S(1)} collective-permute-done((bf16[336,512]{1,0:T(8,128)(2,1)S(1)}, bf16[336,512]{1,0:T(8,128)(2,1)S(1)}, u32[]{:S(2)}, u32[]{:S(2)}) %collective-permute-start.12) | collective-permute-done | bytes 344096 | tf_op jit(solution)/shard_map/ppermute | solution.py:23
  66.7 10.0 %collective-permute-done.13 = bf16[336,512]{1,0:T(8,128)(2,1)} collective-permute-done((bf16[336,512]{1,0:T(8,128)(2,1)S(1)}, bf16[336,512]{1,0:T(8,128)(2,1)}, u32[]{:S(2)}, u32[]{:S(2)}) %collective-permute-start.13) | collective-permute-done | bytes 344096 | tf_op jit(solution)/shard_map/ppermute | solution.py:23
  83.5 9.4 %collective-permute-start.2 = (bf16[128,1024]{1,0:T(8,128)(2,1)}, bf16[128,1024]{1,0:T(8,128)(2,1)}, u32[]{:S(2)}, u32[]{:S(2)}) collective-permute-start(bf16[128,1024]{1,0:T(8,128)(2,1)} %bitcast.3), channel_id=1, source_target_pairs={{0,10},{2,12},{4,14},{1,11},{3,13},{5,15},{16,26},{18,28},{20,30},... | collective-permute-start | bytes 786440 | tf_op jit(solution)/shard_map/ppermute | solution.py:42
  95.1 23.9 %all-reduce.1 = (f32[8]{0:T(128)S(1)}, f32[8]{0:T(128)S(1)}) all-reduce(f32[8]{0:T(128)S(1)} %get-tuple-element.21, f32[8]{0:T(128)S(1)} %get-tuple-element.22), channel_id=1, replica_groups=mesh['grp'=2,'ctx'=8,'pair'=2] {'ctx'}, use_global_device_ids=true, to_apply=%region_1.2 | all-reduce | flops 16 | bytes 128 | tf_op jit(solution)/shard_map/psum | solution.py:83
  126.5 3.3 collective-permute-start.5
  135.7 3.8 %collective-permute-done.5 = bf16[128,1024]{1,0:T(8,128)(2,1)S(1)} collective-permute-done((bf16[128,1024]{1,0:T(8,128)(2,1)}, bf16[128,1024]{1,0:T(8,128)(2,1)S(1)}, u32[]{:S(2)}, u32[]{:S(2)}) %collective-permute-start.5) | collective-permute-done | bytes 262176 | tf_op jit(solution)/shard_map/ppermute | solution.py:42
  139.5 4.1 %collective-permute-done.6 = bf16[128,1024]{1,0:T(8,128)(2,1)S(1)} collective-permute-done((bf16[128,1024]{1,0:T(8,128)(2,1)}, bf16[128,1024]{1,0:T(8,128)(2,1)S(1)}, u32[]{:S(2)}, u32[]{:S(2)}) %collective-permute-start.6) | collective-permute-done | bytes 262176 | tf_op jit(solution)/shard_map/ppermute | solution.py:42
  144.6 4.9 %fusion.15 = bf16[128,1024]{0,1:T(8,128)(2,1)} fusion(f32[128,1024]{0,1:T(8,128)S(1)} %convolution_multiply_fusion.2, bf16[2688,1024]{1,0:T(8,128)(2,1)} %all-gather.2.cloned.1.call-done, bf16[1,128,2688]{2,1,0:T(8,128)(2,1)S(1)} %copy-done), kind=kOutput, calls=%fused_computation.28 | convolution fusion | flops 704905216 | bytes 6979584 | tf_op jit(solution)/shard_map/dot_general | solution.py:73
  154.7 6.5 %collective-permute-start.25 = (bf16[128,1024]{0,1:T(8,128)(2,1)}, bf16[128,1024]{0,1:T(8,128)(2,1)}, u32[]{:S(2)}, u32[]{:S(2)}) collective-permute-start(bf16[128,1024]{0,1:T(8,128)(2,1)} %fusion.15), channel_id=1, source_target_pairs={{0,8},{2,10},{4,12},{6,14},{1,9},{3,11},{5,13},{7,15},{16,24},{18,... | collective-permute-start | bytes 786440 | tf_op jit(solution)/shard_map/ppermute | solution.py:42
  165.3 3.2 copy.60
  168.5 6.9 %fusion.36 = (f32[8,2,128]{2,1,0:T(2,128)S(1)}, f32[8,2,128,1024]{2,3,1,0:T(8,128)}) fusion(pred[128,1024]{0,1:T(8,128)(4,1)} %compare_and_fusion, bf16[1024,8,128,1]{0,2,3,1:T(8,128)(2,1)S(1)} %copy.60, bf16[128,8,2,128]{0,3,2,1:T(8,128)(2,1)S(1)} %bitcast.128), kind=kOutput, calls=%fused_computation.99 | convolution fusion | flops 547357696 | bytes 11149312 | tf_op jit(solution)/shard_map/sub | solution.py:118
  175.4 5.0 %fusion.37 = (bf16[1024,8,128]{0,2,1:T(8,128)(2,1)S(1)}, f32[1024,8,128]{0,2,1:T(8,128)S(1)}) fusion(bf16[128,8,2,128]{3,2,1,0:T(2,128)(2,1)} %reshape_squeeze.7, f32[128]{0:T(128)S(1)} %get-tuple-element.20, f32[8,2,128,1024]{2,3,1,0:T(8,128)} %get-tuple-element.42, f32[8,2,128]{2,1,0:T(2,128)S(1)} %get-tuple-element.41), kind=kOutput, calls=%fused_computation.100 | convolution fusion | flops 544210944 | bytes 15213056 | tf_op jit(solution)/shard_map/jgtl,tjgd->ljd/dot_general | solution.py:134
  206.2 3.4 collective-permute-start.16
  212.8 3.4 fusion.38
  216.5 19.5 %collective-permute-done.17 = bf16[128,1024]{0,1:T(8,128)(2,1)S(1)} collective-permute-done((bf16[128,1024]{0,1:T(8,128)(2,1)S(1)}, bf16[128,1024]{0,1:T(8,128)(2,1)S(1)}, u32[]{:S(2)}, u32[]{:S(2)}) %collective-permute-start.17) | collective-permute-done | bytes 262176 | tf_op jit(solution)/shard_map/ppermute | solution.py:42
  265.4 5.3 %fusion.11 = bf16[1,128,2688]{2,1,0:T(8,128)(2,1)} fusion(f32[128,2688]{1,0:T(8,128)S(1)} %convolution_multiply_fusion, bf16[128,1024]{0,1:T(8,128)(2,1)S(1)} %fusion.27, bf16[2688,1024]{1,0:T(8,128)(2,1)} %all-gather.2.cloned.1.call-done), kind=kOutput, calls=%fused_computation.19 | convolution fusion | flops 705331200 | bytes 7831552 | tf_op jit(solution)/shard_map/tk,dk->td/dot_general | solution.py:152
  270.8 13.4 %collective-permute-done.31 = bf16[128,1024]{1,0:T(8,128)(2,1)} collective-permute-done((bf16[128,1024]{1,0:T(8,128)(2,1)}, bf16[128,1024]{1,0:T(8,128)(2,1)}, u32[]{:S(2)}, u32[]{:S(2)}) %collective-permute-start.31) | collective-permute-done | bytes 262176 | tf_op jit(solution)/shard_map/ppermute | solution.py:42
  284.2 5.1 %collective-permute-done.30 = bf16[128,1024]{1,0:T(8,128)(2,1)S(1)} collective-permute-done((bf16[128,1024]{1,0:T(8,128)(2,1)}, bf16[128,1024]{1,0:T(8,128)(2,1)S(1)}, u32[]{:S(2)}, u32[]{:S(2)}) %collective-permute-start.30) | collective-permute-done | bytes 262176 | tf_op jit(solution)/shard_map/ppermute | solution.py:42
  291.8 73.1 %all-reduce.4.cloned.1.call-done = (f32[2688,16]{0,1:T(8,128)}, f32[16,1024]{1,0:T(8,128)}) async-done(((f32[2688,16]{0,1:T(8,128)}, f32[16,1024]{1,0:T(8,128)}), (f32[2688,16]{0,1:T(8,128)}, f32[16,1024]{1,0:T(8,128)})) %all-reduce.4.cloned.1.call-update) | async-done | bytes 237584 | tf_op jit(solution)/shard_map/psum | solution.py:162
  (160 shorter events, 99.7 us)
Async XLA Ops:
  7.2 137.4 %all-gather.2.cloned.1.call-start = ((), (), s32[]{:S(2)}) async-start(), calls=%async_computation | async-start | bytes 8257536 | tf_op jit(solution)/shard_map/all_gather | solution.py:68
  81.4 283.4 %all-reduce.4.cloned.1.call-start = ((), (), s32[]{:S(2)}) async-start(), calls=%async_computation.1 | async-start | bytes 475136 | tf_op jit(solution)/shard_map/psum | solution.py:162
  81.5 44.3 %collective-permute-start = (bf16[128,1024]{1,0:T(8,128)(2,1)}, bf16[128,1024]{1,0:T(8,128)(2,1)S(1)}, u32[]{:S(2)}, u32[]{:S(2)}) collective-permute-start(bf16[128,1024]{1,0:T(8,128)(2,1)} %bitcast.3), channel_id=1, source_target_pairs={{0,14},{1,15},{16,30},{17,31}} | collective-permute-start | bytes 786440 | tf_op jit(solution)/shard_map/ppermute | solution.py:42
  82.2 48.6 %collective-permute-start.1 = (bf16[128,1024]{1,0:T(8,128)(2,1)}, bf16[128,1024]{1,0:T(8,128)(2,1)}, u32[]{:S(2)}, u32[]{:S(2)}) collective-permute-start(bf16[128,1024]{1,0:T(8,128)(2,1)} %bitcast.3), channel_id=1, source_target_pairs={{0,12},{2,14},{1,13},{3,15},{16,28},{18,30},{17,29},{19,31}} | collective-permute-start | bytes 786440 | tf_op jit(solution)/shard_map/ppermute | solution.py:42
  83.5 50.2 %collective-permute-start.2 = (bf16[128,1024]{1,0:T(8,128)(2,1)}, bf16[128,1024]{1,0:T(8,128)(2,1)}, u32[]{:S(2)}, u32[]{:S(2)}) collective-permute-start(bf16[128,1024]{1,0:T(8,128)(2,1)} %bitcast.3), channel_id=1, source_target_pairs={{0,10},{2,12},{4,14},{1,11},{3,13},{5,15},{16,26},{18,28},{20,30},... | collective-permute-start | bytes 786440 | tf_op jit(solution)/shard_map/ppermute | solution.py:42
  92.9 41.7 %collective-permute-start.3 = (bf16[128,1024]{1,0:T(8,128)(2,1)}, bf16[128,1024]{1,0:T(8,128)(2,1)}, u32[]{:S(2)}, u32[]{:S(2)}) collective-permute-start(bf16[128,1024]{1,0:T(8,128)(2,1)} %bitcast.3), channel_id=1, source_target_pairs={{0,8},{2,10},{4,12},{6,14},{1,9},{3,11},{5,13},{7,15},{16,24},{18,... | collective-permute-start | bytes 786440 | tf_op jit(solution)/shard_map/ppermute | solution.py:42
  149.5 31.5 %collective-permute-start.22 = (bf16[128,1024]{0,1:T(8,128)(2,1)}, bf16[128,1024]{0,1:T(8,128)(2,1)}, u32[]{:S(2)}, u32[]{:S(2)}) collective-permute-start(bf16[128,1024]{0,1:T(8,128)(2,1)} %fusion.15), channel_id=1, source_target_pairs={{0,14},{1,15},{16,30},{17,31}} | collective-permute-start | bytes 786440 | tf_op jit(solution)/shard_map/ppermute | solution.py:42
  151.0 34.0 %collective-permute-start.23 = (bf16[128,1024]{0,1:T(8,128)(2,1)}, bf16[128,1024]{0,1:T(8,128)(2,1)}, u32[]{:S(2)}, u32[]{:S(2)}) collective-permute-start(bf16[128,1024]{0,1:T(8,128)(2,1)} %fusion.15), channel_id=1, source_target_pairs={{0,12},{2,14},{1,13},{3,15},{16,28},{18,30},{17,29},{19,31}} | collective-permute-start | bytes 786440 | tf_op jit(solution)/shard_map/ppermute | solution.py:42
  152.4 35.6 %collective-permute-start.24 = (bf16[128,1024]{0,1:T(8,128)(2,1)}, bf16[128,1024]{0,1:T(8,128)(2,1)}, u32[]{:S(2)}, u32[]{:S(2)}) collective-permute-start(bf16[128,1024]{0,1:T(8,128)(2,1)} %fusion.15), channel_id=1, source_target_pairs={{0,10},{2,12},{4,14},{1,11},{3,13},{5,15},{16,26},{18,28},{20,30},... | collective-permute-start | bytes 786440 | tf_op jit(solution)/shard_map/ppermute | solution.py:42
  154.7 35.0 %collective-permute-start.25 = (bf16[128,1024]{0,1:T(8,128)(2,1)}, bf16[128,1024]{0,1:T(8,128)(2,1)}, u32[]{:S(2)}, u32[]{:S(2)}) collective-permute-start(bf16[128,1024]{0,1:T(8,128)(2,1)} %fusion.15), channel_id=1, source_target_pairs={{0,8},{2,10},{4,12},{6,14},{1,9},{3,11},{5,13},{7,15},{16,24},{18,... | collective-permute-start | bytes 786440 | tf_op jit(solution)/shard_map/ppermute | solution.py:42
  161.3 30.4 %collective-permute-start.26 = (bf16[128,1024]{0,1:T(8,128)(2,1)}, bf16[128,1024]{0,1:T(8,128)(2,1)}, u32[]{:S(2)}, u32[]{:S(2)}) collective-permute-start(bf16[128,1024]{0,1:T(8,128)(2,1)} %fusion.15), channel_id=1, source_target_pairs={{0,6},{2,8},{4,10},{6,12},{8,14},{1,7},{3,9},{5,11},{7,13},{9,15},... | collective-permute-start | bytes 786440 | tf_op jit(solution)/shard_map/ppermute | solution.py:42
  188.0 18.2 %collective-permute-start.21 = (bf16[128,1024]{0,1:T(8,128)(2,1)S(1)}, bf16[128,1024]{0,1:T(8,128)(2,1)S(1)}, u32[]{:S(2)}, u32[]{:S(2)}) collective-permute-start(bf16[128,1024]{0,1:T(8,128)(2,1)S(1)} %bitcast.143), channel_id=1, source_target_pairs={{14,0},{15,1},{30,16},{31,17}} | collective-permute-start | bytes 786440 | tf_op jit(solution)/shard_map/ppermute | solution.py:42
  189.7 19.9 %collective-permute-start.20 = (bf16[128,1024]{0,1:T(8,128)(2,1)S(1)}, bf16[128,1024]{0,1:T(8,128)(2,1)S(1)}, u32[]{:S(2)}, u32[]{:S(2)}) collective-permute-start(bf16[128,1024]{0,1:T(8,128)(2,1)S(1)} %bitcast.142), channel_id=1, source_target_pairs={{12,0},{14,2},{13,1},{15,3},{28,16},{30,18},{29,17},{31,19}} | collective-permute-start | bytes 786440 | tf_op jit(solution)/shard_map/ppermute | solution.py:42
  191.6 24.6 %collective-permute-start.19 = (bf16[128,1024]{0,1:T(8,128)(2,1)S(1)}, bf16[128,1024]{0,1:T(8,128)(2,1)S(1)}, u32[]{:S(2)}, u32[]{:S(2)}) collective-permute-start(bf16[128,1024]{0,1:T(8,128)(2,1)S(1)} %bitcast.141), channel_id=1, source_target_pairs={{10,0},{12,2},{14,4},{11,1},{13,3},{15,5},{26,16},{28,18},{30,20},... | collective-permute-start | bytes 786440 | tf_op jit(solution)/shard_map/ppermute | solution.py:42
  197.1 19.4 %collective-permute-start.18 = (bf16[128,1024]{0,1:T(8,128)(2,1)S(1)}, bf16[128,1024]{0,1:T(8,128)(2,1)S(1)}, u32[]{:S(2)}, u32[]{:S(2)}) collective-permute-start(bf16[128,1024]{0,1:T(8,128)(2,1)S(1)} %bitcast.140), channel_id=1, source_target_pairs={{8,0},{10,2},{12,4},{14,6},{9,1},{11,3},{13,5},{15,7},{24,16},{26,... | collective-permute-start | bytes 786440 | tf_op jit(solution)/shard_map/ppermute | solution.py:42
  198.5 37.6 %collective-permute-start.17 = (bf16[128,1024]{0,1:T(8,128)(2,1)S(1)}, bf16[128,1024]{0,1:T(8,128)(2,1)S(1)}, u32[]{:S(2)}, u32[]{:S(2)}) collective-permute-start(bf16[128,1024]{0,1:T(8,128)(2,1)S(1)} %bitcast.139), channel_id=1, source_target_pairs={{6,0},{8,2},{10,4},{12,6},{14,8},{7,1},{9,3},{11,5},{13,7},{15,9},... | collective-permute-start | bytes 786440 | tf_op jit(solution)/shard_map/ppermute | solution.py:42
  206.2 31.3 %collective-permute-start.16 = (bf16[128,1024]{0,1:T(8,128)(2,1)S(1)}, bf16[128,1024]{0,1:T(8,128)(2,1)S(1)}, u32[]{:S(2)}, u32[]{:S(2)}) collective-permute-start(bf16[128,1024]{0,1:T(8,128)(2,1)S(1)} %bitcast.138), channel_id=1, source_target_pairs={{4,0},{6,2},{8,4},{10,6},{12,8},{14,10},{5,1},{7,3},{9,5},{11,7},{... | collective-permute-start | bytes 786440 | tf_op jit(solution)/shard_map/ppermute | solution.py:42
  209.6 27.9 %collective-permute-start.15 = (bf16[128,1024]{0,1:T(8,128)(2,1)S(1)}, bf16[128,1024]{0,1:T(8,128)(2,1)S(1)}, u32[]{:S(2)}, u32[]{:S(2)}) collective-permute-start(bf16[128,1024]{0,1:T(8,128)(2,1)S(1)} %bitcast.137), channel_id=1, source_target_pairs={{2,0},{4,2},{6,4},{8,6},{10,8},{12,10},{14,12},{3,1},{5,3},{7,5},{... | collective-permute-start | bytes 786440 | tf_op jit(solution)/shard_map/ppermute | solution.py:42
  244.0 17.6 %collective-permute-start.35 = (bf16[128,1024]{1,0:T(8,128)(2,1)}, bf16[128,1024]{1,0:T(8,128)(2,1)S(1)}, u32[]{:S(2)}, u32[]{:S(2)}) collective-permute-start(bf16[128,1024]{1,0:T(8,128)(2,1)} %copy.53), channel_id=1, source_target_pairs={{14,0},{15,1},{30,16},{31,17}} | collective-permute-start | bytes 786440 | tf_op jit(solution)/shard_map/ppermute | solution.py:42
  248.9 21.8 %collective-permute-start.33 = (bf16[128,1024]{1,0:T(8,128)(2,1)}, bf16[128,1024]{1,0:T(8,128)(2,1)S(1)}, u32[]{:S(2)}, u32[]{:S(2)}) collective-permute-start(bf16[128,1024]{1,0:T(8,128)(2,1)} %copy.51), channel_id=1, source_target_pairs={{10,0},{12,2},{14,4},{11,1},{13,3},{15,5},{26,16},{28,18},{30,20},... | collective-permute-start | bytes 786440 | tf_op jit(solution)/shard_map/ppermute | solution.py:42
  252.9 17.9 %collective-permute-start.32 = (bf16[128,1024]{1,0:T(8,128)(2,1)}, bf16[128,1024]{1,0:T(8,128)(2,1)S(1)}, u32[]{:S(2)}, u32[]{:S(2)}) collective-permute-start(bf16[128,1024]{1,0:T(8,128)(2,1)} %copy.50), channel_id=1, source_target_pairs={{8,0},{10,2},{12,4},{14,6},{9,1},{11,3},{13,5},{15,7},{24,16},{26,... | collective-permute-start | bytes 786440 | tf_op jit(solution)/shard_map/ppermute | solution.py:42
  256.0 28.2 %collective-permute-start.31 = (bf16[128,1024]{1,0:T(8,128)(2,1)}, bf16[128,1024]{1,0:T(8,128)(2,1)}, u32[]{:S(2)}, u32[]{:S(2)}) collective-permute-start(bf16[128,1024]{1,0:T(8,128)(2,1)} %copy.49), channel_id=1, source_target_pairs={{6,0},{8,2},{10,4},{12,6},{14,8},{7,1},{9,3},{11,5},{13,7},{15,9},... | collective-permute-start | bytes 786440 | tf_op jit(solution)/shard_map/ppermute | solution.py:42
  261.6 27.7 %collective-permute-start.30 = (bf16[128,1024]{1,0:T(8,128)(2,1)}, bf16[128,1024]{1,0:T(8,128)(2,1)S(1)}, u32[]{:S(2)}, u32[]{:S(2)}) collective-permute-start(bf16[128,1024]{1,0:T(8,128)(2,1)} %copy.48), channel_id=1, source_target_pairs={{4,0},{6,2},{8,4},{10,6},{12,8},{14,10},{5,1},{7,3},{9,5},{11,7},{... | collective-permute-start | bytes 786440 | tf_op jit(solution)/shard_map/ppermute | solution.py:42
  263.5 26.3 %collective-permute-start.29 = (bf16[128,1024]{1,0:T(8,128)(2,1)}, bf16[128,1024]{1,0:T(8,128)(2,1)S(1)}, u32[]{:S(2)}, u32[]{:S(2)}) collective-permute-start(bf16[128,1024]{1,0:T(8,128)(2,1)} %copy.46), channel_id=1, source_target_pairs={{2,0},{4,2},{6,4},{8,6},{10,8},{12,10},{14,12},{3,1},{5,3},{7,5},{... | collective-permute-start | bytes 786440 | tf_op jit(solution)/shard_map/ppermute | solution.py:42
  (27 other events, 616.9 us)
Sparse Core Ops, SparseCore 0:
  81.6 20.7 all-gather.1
  261.3 103.5 all-reduce.3
